TPU v7x, 256 devices: a whole 4x4x8 slice. The times are simulated.
256 devices in a mesh: obs: 4 (over y), blk: 64 (over x, z, core).
Axes of the slice: x: 4, y: 4, z: 8, core: 2. Of those that a mesh axis runs over, the one named last changes fastest.
Arguments:
- design_tiles: float32 [32768, 8, 128], P(('obs', 'blk')), may hold values from -8 to 8
- block_ids: int32 [32768, 8], P(('obs', 'blk')), may hold values from 0 to 63, as said below
- obs_weight: float32 [32768], P(('obs', 'blk')), may hold values from 4.8828126e-05 to 0.00048828125
- block_owner: int32 [64], replicated, may hold values from 0 to 63, each once
- prior_weight: float32 [512], replicated, may hold values from 0.25 to 1
Outputs:
- panel_factor: float32 [8192, 256], P('blk')
- panel_update: float32 [8192, 256], P('blk')
Inputs may be any that keep to these rules, and one draw needn't show every extreme that they name: `block_ids`: the 8 blocks of an observation are distinct. Among the 128 observations of one device (aligned blocks of rows) no block is named by more than 24 of them, and in every draw some device has a block named by exactly 24. `block_owner`: A permutation: each owner index once.
All inputs are finite; a program needn't handle non-finite values.
Results may differ from a plain program's by a relative error of at most 0.0003.
Values sent between devices are 32-bit elements; how exact they have to be, the bound alone decides.
No kernel may reach another device: no remote copies, remote signals or barrier semaphores. Data moves between devices by JAX's collectives and lax.ppermute only.
A program may use at most 64 MiB of HBM per device.

v0:
```python
import jax
import jax.numpy as jnp
from jax import lax
from jax.sharding import PartitionSpec as P


def back_solve(factor, right_rows):
    return jax.scipy.linalg.solve_triangular(factor, right_rows.T, lower=True).T


def with_prior(owned, row_index, prior_weight):
    col_index = jnp.arange(prior_weight.shape[0], dtype=jnp.int32)
    return owned + jnp.where(col_index[None, :] == row_index[:, None], prior_weight[None, :], 0.0)


def placed_square(owned, row_index, panel_cols):
    col_index = jnp.arange(panel_cols, dtype=jnp.int32)
    placing = (row_index[:, None] == col_index[None, :]).astype(jnp.float32)
    return jnp.einsum("rq,rp->qp", placing, owned, precision=lax.Precision.HIGHEST)


def finish_rows(owned, square, half_cols):
    mirrored = 0.5 * (square + square.T)
    factor = jnp.linalg.cholesky(mirrored[:half_cols, :half_cols])
    coupling = back_solve(factor, mirrored[half_cols:, :half_cols])
    first_rows = back_solve(factor, owned[:, :half_cols])
    update_rows = owned[:, half_cols:] - jnp.dot(
        first_rows, coupling.T, precision=lax.Precision.HIGHEST, preferred_element_type=jnp.float32
    )
    return (first_rows, update_rows)


def select_columns(labels, design_tiles, wanted):
    touched = design_tiles.shape[1]
    columns = jnp.zeros(
        (design_tiles.shape[0], wanted.shape[0], design_tiles.shape[2]), jnp.float32
    )
    for entry in range(touched):
        hit = labels[:, entry, None] == wanted[None, :]
        columns = columns + jnp.where(hit[:, :, None], design_tiles[:, entry, None, :], 0.0)
    return columns.reshape(design_tiles.shape[0], wanted.shape[0] * design_tiles.shape[2])


def local(design_tiles, block_ids, obs_weight, block_owner, prior_weight):
    block_width = design_tiles.shape[2]
    block_count = block_owner.shape[0]
    panel_cols = prior_weight.shape[0]
    half_cols = panel_cols // 2
    panel_blocks = panel_cols // block_width
    block_range = jnp.arange(block_count, dtype=jnp.int32)
    owner_index = lax.axis_index("blk")
    owner_block = jnp.sum(jnp.where(block_owner == owner_index, block_range, 0))
    slots = jnp.sum(
        jnp.where(
            block_ids[:, :, None] == block_range[None, None, :], block_owner[None, None, :], 0
        ),
        axis=2,
    )
    panel_design = select_columns(
        block_ids, design_tiles, jnp.arange(panel_blocks, dtype=jnp.int32)
    )
    weighted = panel_design * obs_weight[:, None]
    wanted = jnp.arange(lax.axis_size("blk") * block_width // block_width, dtype=jnp.int32)
    columns = select_columns(slots, design_tiles, wanted)
    partial_value = lax.psum_scatter(
        jnp.einsum("oi,op->ip", columns, weighted, precision=lax.Precision.HIGHEST),
        "blk",
        scatter_dimension=0,
        tiled=True,
    )
    owned = lax.psum(partial_value, "obs")
    row_index = owner_block * block_width + jnp.arange(block_width, dtype=jnp.int32)
    owned = with_prior(owned, row_index, prior_weight)
    square = lax.psum(placed_square(owned, row_index, panel_cols), "blk")
    first_rows, update_rows = finish_rows(owned, square, half_cols)
    return (first_rows, update_rows)


def solution(mesh):
    in_specs = (P(("obs", "blk"), None, None), P(("obs", "blk"), None), P(("obs", "blk")), P(), P())
    out_specs = (P("blk", None), P("blk", None))
    return jax.shard_map(local, mesh=mesh, in_specs=in_specs, out_specs=out_specs, check_vma=False)
```

profile of v0, /device:TPU:8, one launch (start us, length us, event | category | flops | bytes accessed | tf_op | source)
XLA Modules:
  0.0 547.7 jit_solution(13729939461648007592)
XLA Ops:
  7.2 1.0 slice_bitcast_fusion.15
  8.2 0.8 select_reduce_fusion
  9.0 3.5 fusion.27
  13.4 9.0 %select_add_fusion = f32[128,64,128]{2,1,0:T(8,128)S(1)} fusion(f32[128,128]{1,0:T(8,128)S(1)} %bitcast.108, f32[128,128]{1,0:T(8,128)S(1)} %bitcast.110, f32[128,128]{1,0:T(8,128)S(1)} %bitcast.98, f32[128,128]{1,0:T(8,128)S(1)} %bitcast.100, f32[128,128]{1,0:T(8,128)S(1)} %bitcast.102, f32[128,128]{1,0:T(8,128)S(1)} %bitcast.104, ...), kind=kLoop, calls=%fused_computation.5 | loop fusion | flops 15728640 | bytes 4784128 | tf_op jit(solution)/shard_map/add | solution.py:40
  22.4 1.6 add_multiply_fusion
  23.9 18.2 %fusion = f32[8192,512]{1,0:T(8,128)} fusion(f32[16,8,64,128]{3,2,1,0:T(8,128)S(1)} %bitcast.94, f32[16,8,4,128]{3,2,1,0:T(4,128)S(1)} %bitcast.95), kind=kOutput, calls=%fused_computation.2 | convolution fusion | flops 6442450944 | bytes 21233664 | tf_op jit(solution)/shard_map/oi,op->ip/dot_general | solution.py:66
  42.2 192.8 %reduce-scatter.2.cloned.1.call-done = f32[128,512]{1,0:T(8,128)} async-done(((f32[8192,512]{1,0:T(8,128)}), f32[128,512]{1,0:T(8,128)}) %reduce-scatter.2.cloned.1.call-update) | async-done | bytes 262160 | tf_op jit(solution)/shard_map/reduce_scatter | solution.py:65
  236.6 45.1 %all-reduce.4.cloned.1.call-done = f32[128,512]{1,0:T(8,128)} async-done(((f32[128,512]{1,0:T(8,128)}), f32[128,512]{1,0:T(8,128)}) %all-reduce.4.cloned.1.call-update) | async-done | bytes 262160 | tf_op jit(solution)/shard_map/psum | solution.py:71
  281.7 1.0 select_add_fusion.1
  282.8 1.7 fusion.10
  284.5 189.4 %all-reduce.6.cloned.1.call-done = f32[512,512]{1,0:T(8,128)} async-done(((f32[512,512]{1,0:T(8,128)}), f32[512,512]{1,0:T(8,128)}) %all-reduce.6.cloned.1.call-update) | async-done | bytes 1048592 | tf_op jit(solution)/shard_map/psum | solution.py:74
  474.0 1.6 copy.11
  475.5 1.4 fusion.3
  477.2 11.7 %cholesky.50 = f32[128,128]{1,0:T(8,128)S(1)} custom-call(f32[128,128]{1,0:T(8,128)S(1)} %cholesky.118), custom_call_target="Cholesky" | custom-call | tf_op jit(solution)/shard_map/jit(cholesky)/cholesky | solution.py:24
  489.0 9.8 %custom-call.18 = f32[1,128,128]{1,2,0:T(8,128)S(1)} custom-call(f32[1,128,128]{2,1,0:T(8,128)S(1)} %get-tuple-element.37), custom_call_target="InvertDiagBlocksLowerTriangular" | custom-call | tf_op jit(solution)/shard_map/jit(cholesky)/cholesky | solution.py:24
  499.3 11.7 %cholesky.105 = f32[128,128]{1,0:T(8,128)S(1)} custom-call(f32[128,128]{1,0:T(8,128)S(1)} %convolution_subtract_fusion.3), custom_call_target="Cholesky" | custom-call | tf_op jit(solution)/shard_map/jit(cholesky)/cholesky | solution.py:24
  511.0 0.7 compare_reduce_fusion
  511.7 0.6 compare_reduce_fusion.1
  513.8 4.1 while.1
  514.5 1.4 bitcast_dynamic-update-slice_fusion.2
  516.5 1.4 bitcast_dynamic-update-slice_fusion.2
  517.9 19.7 %custom-call.19 = f32[2,128,128]{1,2,0:T(8,128)S(1)} custom-call(f32[2,128,128]{2,1,0:T(8,128)S(1)} %get-tuple-element.9), custom_call_target="InvertDiagBlocksLowerTriangular" | custom-call | tf_op jit(solution)/shard_map/jit(_solve_triangular)/triangular_solve | solution.py:8
  539.4 1.1 convolution_subtract_fusion
  540.4 0.8 copy.13
  (48 shorter events, 5.6 us)
Async XLA Ops:
  7.2 15.2 %copy-start.1 = (f32[128]{0:T(128)S(1)}, f32[128]{0:T(128)}, u32[]{:S(2)}) copy-start(f32[128]{0:T(128)} %param.7) | copy-start | bytes 1540
  7.2 227.8 %reduce-scatter.2.cloned.1.call-start = ((), (), s32[]{:S(2)}) async-start(), calls=%async_computation.1 | async-start | bytes 17039360 | tf_op jit(solution)/shard_map/reduce_scatter | solution.py:65
  42.1 193.2 %copy-start.2 = (s32[64]{0:T(128)S(1)}, s32[64]{0:T(128)}, u32[]{:S(2)}) copy-start(s32[64]{0:T(128)} %param.8) | copy-start | bytes 772
  42.1 239.6 %copy-start = (f32[512]{0:T(512)S(1)}, f32[512]{0:T(512)}, u32[]{:S(2)}) copy-start(f32[512]{0:T(512)} %param.9) | copy-start | bytes 6148
  42.2 239.6 %all-reduce.4.cloned.1.call-start = ((), (), s32[]{:S(2)}) async-start(), calls=%async_computation.2 | async-start | bytes 524288 | tf_op jit(solution)/shard_map/psum | solution.py:71
  235.0 238.9 %all-reduce.6.cloned.1.call-start = ((), (), s32[]{:S(2)}) async-start(), calls=%async_computation.3 | async-start | bytes 2097152 | tf_op jit(solution)/shard_map/psum | solution.py:74
Sparse Core Ops, SparseCore 0:
  42.3 192.7 reduce-scatter.1
  237.3 44.3 all-reduce.3
  285.1 188.7 all-reduce.5
where the time goes:
time: 548 us
  waiting for transfers between devices  427 us (78%)
  other arithmetic  69.7 us (13%)
  matrix products  23.1 us (4%)
  between operations  16 us (3%)
  local copies, waits for them, and re-layouts  11 us (2%)
    reduce_scatter x1, waiting for transfers between devices, local(): lax.psum_scatter(jnp.einsum('oi,op->ip', columns, weighted, precision=lax...  193 us
    psum x1, waiting for transfers between devices, local(): square = lax.psum(placed_square(owned, row_index, panel_cols), 'blk')  189 us
    psum x1, waiting for transfers between devices, local(): owned = lax.psum(partial_value, 'obs')  45.1 us
    another operation x7, other arithmetic, finish_rows(): factor = jnp.linalg.cholesky(mirrored[:half_cols, :half_cols])  34.6 us
    another operation x3, other arithmetic, back_solve(): return jax.scipy.linalg.solve_triangular(factor, right_rows.T, lower=True).T  19.7 us
    dot_general x1, matrix products, local(): jnp.einsum('oi,op->ip', columns, weighted, precision=lax.Precision.HIGHEST)  18.2 us
  transfers between devices with their start and end apart: 3, of which 3 were waited for; matrix products, arithmetic and copies ran while one was open for 0% of the time, Pallas kernels for 0%

commit v1 on v0

--- a/solution.py
+++ b/solution.py
@@ -68,7 +68,9 @@
         scatter_dimension=0,
         tiled=True,
     )
-    owned = lax.psum(partial_value, "obs")
+    owned = partial_value
+    for hop in (1, 2):
+        owned = owned + lax.ppermute(owned, "obs", [(dev, dev ^ hop) for dev in range(4)])
     row_index = owner_block * block_width + jnp.arange(block_width, dtype=jnp.int32)
     owned = with_prior(owned, row_index, prior_weight)
     square = lax.psum(placed_square(owned, row_index, panel_cols), "blk")

time: 548 us -> 514 us (0.938)
  waiting for transfers between devices: 427 us -> 389 us
    psum x1 -> x0, waiting for transfers between devices: 45.1 us -> none  [local(): owned = lax.psum(partial_value, 'obs')]
    ppermute x0 -> x2, waiting for transfers between devices: none -> 9.13 us  [local(): lax.ppermute(owned, 'obs', [(dev, dev ^ hop) for dev in range(4)])]
  transfers between devices with their start and end apart: 3 -> 4, of which waited for: 3 -> 4; matrix products, arithmetic and copies ran while one was open for 0% -> 0% of each run, Pallas kernels for 0% -> 0%
where the time goes in v1:
time: 514 us
  waiting for transfers between devices  389 us (76%)
  other arithmetic  69.7 us (14%)
  matrix products  23.1 us (4%)
  between operations  16.2 us (3%)
  local copies, waits for them, and re-layouts  11 us (2%)
    reduce_scatter x1, waiting for transfers between devices, local(): lax.psum_scatter(jnp.einsum('oi,op->ip', columns, weighted, precision=lax...  193 us
    psum x1, waiting for transfers between devices, local(): square = lax.psum(placed_square(owned, row_index, panel_cols), 'blk')  187 us
    another operation x7, other arithmetic, finish_rows(): factor = jnp.linalg.cholesky(mirrored[:half_cols, :half_cols])  34.6 us
    another operation x3, other arithmetic, back_solve(): return jax.scipy.linalg.solve_triangular(factor, right_rows.T, lower=True).T  19.7 us
    dot_general x1, matrix products, local(): jnp.einsum('oi,op->ip', columns, weighted, precision=lax.Precision.HIGHEST)  18.2 us
  transfers between devices with their start and end apart: 4, of which 4 were waited for; matrix products, arithmetic and copies ran while one was open for 0% of the time, Pallas kernels for 0%

profile of v1, /device:TPU:8, one launch (start us, length us, event | category | flops | bytes accessed | tf_op | source)
XLA Modules:
  0.0 513.9 jit_solution(6014039921650060898)
XLA Ops:
  7.2 1.0 slice_bitcast_fusion.15
  8.2 0.8 select_reduce_fusion
  9.0 3.5 fusion.31
  13.4 9.0 %select_add_fusion = f32[128,64,128]{2,1,0:T(8,128)S(1)} fusion(f32[128,128]{1,0:T(8,128)S(1)} %bitcast.107, f32[128,128]{1,0:T(8,128)S(1)} %bitcast.109, f32[128,128]{1,0:T(8,128)S(1)} %bitcast.97, f32[128,128]{1,0:T(8,128)S(1)} %bitcast.99, f32[128,128]{1,0:T(8,128)S(1)} %bitcast.101, f32[128,128]{1,0:T(8,128)S(1)} %bitcast.103, ...), kind=kLoop, calls=%fused_computation.5 | loop fusion | flops 15728640 | bytes 4784128 | tf_op jit(solution)/shard_map/add | solution.py:40
  22.4 1.6 add_multiply_fusion
  23.9 18.2 %fusion = f32[8192,512]{1,0:T(8,128)} fusion(f32[16,8,64,128]{3,2,1,0:T(8,128)S(1)} %bitcast.93, f32[16,8,4,128]{3,2,1,0:T(4,128)S(1)} %bitcast.94), kind=kOutput, calls=%fused_computation.2 | convolution fusion | flops 6442450944 | bytes 21233664 | tf_op jit(solution)/shard_map/oi,op->ip/dot_general | solution.py:66
  42.2 192.7 %reduce-scatter.2.cloned.1.call-done = f32[128,512]{1,0:T(8,128)} async-done(((f32[8192,512]{1,0:T(8,128)}), f32[128,512]{1,0:T(8,128)}) %reduce-scatter.2.cloned.1.call-update) | async-done | bytes 262160 | tf_op jit(solution)/shard_map/reduce_scatter | solution.py:65
  235.4 6.1 %collective-permute-done = f32[128,512]{1,0:T(8,128)S(1)} collective-permute-done((f32[128,512]{1,0:T(8,128)}, f32[128,512]{1,0:T(8,128)S(1)}, u32[]{:S(2)}, u32[]{:S(2)}) %collective-permute-start) | collective-permute-done | bytes 262176 | tf_op jit(solution)/shard_map/ppermute | solution.py:73
  241.5 1.0 add.225
  242.5 4.5 collective-permute-start.1
  248.3 3.1 collective-permute-done.1
  251.4 1.7 fusion.11
  253.2 186.7 %all-reduce.3.cloned.1.call-done = f32[512,512]{1,0:T(8,128)} async-done(((f32[512,512]{1,0:T(8,128)}), f32[512,512]{1,0:T(8,128)}) %all-reduce.3.cloned.1.call-update) | async-done | bytes 1048592 | tf_op jit(solution)/shard_map/psum | solution.py:76
  439.9 1.6 copy.11
  441.5 1.4 fusion.3
  443.2 11.7 %cholesky.50 = f32[128,128]{1,0:T(8,128)S(1)} custom-call(f32[128,128]{1,0:T(8,128)S(1)} %cholesky.118), custom_call_target="Cholesky" | custom-call | tf_op jit(solution)/shard_map/jit(cholesky)/cholesky | solution.py:24
  455.0 9.8 %custom-call.18 = f32[1,128,128]{1,2,0:T(8,128)S(1)} custom-call(f32[1,128,128]{2,1,0:T(8,128)S(1)} %get-tuple-element.37), custom_call_target="InvertDiagBlocksLowerTriangular" | custom-call | tf_op jit(solution)/shard_map/jit(cholesky)/cholesky | solution.py:24
  465.3 11.7 %cholesky.105 = f32[128,128]{1,0:T(8,128)S(1)} custom-call(f32[128,128]{1,0:T(8,128)S(1)} %convolution_subtract_fusion.1), custom_call_target="Cholesky" | custom-call | tf_op jit(solution)/shard_map/jit(cholesky)/cholesky | solution.py:24
  479.7 4.1 while.1
  480.5 1.4 bitcast_dynamic-update-slice_fusion.2
  482.4 1.4 bitcast_dynamic-update-slice_fusion.2
  483.8 19.7 %custom-call.19 = f32[2,128,128]{1,2,0:T(8,128)S(1)} custom-call(f32[2,128,128]{2,1,0:T(8,128)S(1)} %get-tuple-element.9), custom_call_target="InvertDiagBlocksLowerTriangular" | custom-call | tf_op jit(solution)/shard_map/jit(_solve_triangular)/triangular_solve | solution.py:8
  505.3 1.1 slice_subtract_fusion
  506.3 0.8 copy.13
  (50 shorter events, 7.3 us)
Async XLA Ops:
  7.2 15.2 %copy-start.1 = (f32[128]{0:T(128)S(1)}, f32[128]{0:T(128)}, u32[]{:S(2)}) copy-start(f32[128]{0:T(128)} %param.7) | copy-start | bytes 1540
  7.2 227.7 %reduce-scatter.2.cloned.1.call-start = ((), (), s32[]{:S(2)}) async-start(), calls=%async_computation.1 | async-start | bytes 17039360 | tf_op jit(solution)/shard_map/reduce_scatter | solution.py:65
  42.1 204.9 %copy-start.2 = (s32[64]{0:T(128)S(1)}, s32[64]{0:T(128)}, u32[]{:S(2)}) copy-start(s32[64]{0:T(128)} %param.8) | copy-start | bytes 772
  42.1 209.2 %copy-start = (f32[512]{0:T(512)S(1)}, f32[512]{0:T(512)}, u32[]{:S(2)}) copy-start(f32[512]{0:T(512)} %param.9) | copy-start | bytes 6148
  42.1 397.8 %all-reduce.3.cloned.1.call-start = ((), (), s32[]{:S(2)}) async-start(), calls=%async_computation.2 | async-start | bytes 2097152 | tf_op jit(solution)/shard_map/psum | solution.py:76
  234.9 6.6 %collective-permute-start = (f32[128,512]{1,0:T(8,128)}, f32[128,512]{1,0:T(8,128)S(1)}, u32[]{:S(2)}, u32[]{:S(2)}) collective-permute-start(f32[128,512]{1,0:T(8,128)} %reduce-scatter.2.cloned.1.call-done), channel_id=1, source_target_pairs={{0,64},{64,0},{128,192},{192,128},{1,65},{65,1},{129,193},{193,129... | collective-permute-start | bytes 786440 | tf_op jit(solution)/shard_map/ppermute | solution.py:73
  242.5 8.8 %collective-permute-start.1 = (f32[128,512]{1,0:T(8,128)S(1)}, f32[128,512]{1,0:T(8,128)S(1)}, u32[]{:S(2)}, u32[]{:S(2)}) collective-permute-start(f32[128,512]{1,0:T(8,128)S(1)} %add.225), channel_id=1, source_target_pairs={{0,128},{64,192},{128,0},{192,64},{1,129},{65,193},{129,1},{193,65... | collective-permute-start | bytes 786440 | tf_op jit(solution)/shard_map/ppermute | solution.py:73
Sparse Core Ops, SparseCore 0:
  42.3 192.5 reduce-scatter.1
  253.3 186.6 all-reduce.2
